TPU v7x, 32 devices: a whole 2x2x4 slice. The times are simulated.
32 devices in a mesh: shard: 4 (over z), rep: 8 (over y, x, core).
Axes of the slice: x: 2, y: 2, z: 4, core: 2. Of those that a mesh axis runs over, the one named last changes fastest.
Arguments:
- grads: bfloat16 [1, 8192, 28672], P(None, 'shard', 'rep'), may hold values from -81 to 81
- seeds: int32 [1], replicated, may hold values from 0 to 999999
Outputs:
- projected: bfloat16 [512, 1, 28672], P('shard', None, 'rep')
All inputs are finite; a program needn't handle non-finite values.
Results may differ from a plain program's by a relative error of at most 0.0056.
Values may be sent and summed in bfloat16 or wider, within the bound.
No kernel may reach another device: no remote copies, remote signals or barrier semaphores. Data moves between devices by JAX's collectives and lax.ppermute only.
A program may use at most 128 MiB of HBM per device.

v0:
```python
import jax
import jax.numpy as jnp
from jax import lax
from jax.sharding import PartitionSpec as P

RANK = 512
mix_first = 668265263
mix_second = -2048144789
mix_third = -1028477387


def sketch_table(seeds, first_row, count, rank):
    rows = first_row + lax.iota(jnp.int32, count)
    columns = lax.iota(jnp.int32, rank)
    counter = rows[:, None] * jnp.int32(rank) + columns[None, :]
    hashed = jnp.bitwise_xor(counter[None, :, :], (seeds * jnp.int32(mix_first))[:, None, None])
    hashed = hashed * jnp.int32(mix_second)
    hashed = jnp.bitwise_xor(hashed, lax.shift_right_logical(hashed, jnp.int32(15)))
    hashed = hashed * jnp.int32(mix_third)
    hashed = jnp.bitwise_xor(hashed, lax.shift_right_logical(hashed, jnp.int32(13)))
    unit = lax.shift_right_logical(hashed, jnp.int32(8)).astype(jnp.float32) * (1.0 / 16777216.0)
    return (2.0 * unit - 1.0).astype(jnp.bfloat16)


def body(grads, seeds):
    mats, depth, width = grads.shape
    col0 = lax.axis_index("rep") * width
    outs = []
    for m in range(mats):
        table = sketch_table(seeds[m : m + 1], col0, width, RANK)[0]
        g = grads[m]
        partial = jnp.dot(g, table, preferred_element_type=jnp.float32)
        sketch_rows = lax.psum(partial, "rep")
        local_gram = jnp.dot(
            sketch_rows.T,
            sketch_rows,
            precision=lax.Precision.HIGHEST,
            preferred_element_type=jnp.float32,
        )
        gram = lax.psum(local_gram, "shard")
        factor = jnp.linalg.cholesky(gram)
        basis_rows = lax.linalg.triangular_solve(
            factor, sketch_rows, left_side=False, lower=True, transpose_a=True
        ).astype(jnp.bfloat16)
        partial_sum = jnp.dot(basis_rows.T, g, preferred_element_type=jnp.float32)
        outs.append(partial_sum)
    partial_sum = jnp.stack(outs, axis=1).astype(jnp.bfloat16)
    return lax.psum_scatter(partial_sum, "shard", scatter_dimension=0, tiled=True)


def solution(mesh):
    return jax.shard_map(
        body,
        mesh=mesh,
        in_specs=(P(None, "shard", "rep"), P()),
        out_specs=P("shard", None, "rep"),
        check_vma=False,
    )
```

profile of v0, /device:TPU:0, one launch (start us, length us, event | category | flops | bytes accessed | tf_op | source)
XLA Modules:
  0.0 411.4 jit_solution(13956208684615322948)
XLA Ops:
  7.2 16.7 %fusion.27 = f32[2048,512]{0,1:T(8,128)} fusion(bf16[1,2048,3584]{2,1,0:T(8,128)(2,1)} %param.2, s32[]{:T(128)} %bitcast, s32[3584]{0:T(1024)S(1)} %add_multiply_fusion), kind=kOutput, calls=%fused_computation.26 | convolution fusion | flops 7540047872 | bytes 18888708 | tf_op jit(solution)/shard_map/dot_general | solution.py:32
  23.9 0.3 all-reduce.6.cloned.1.call-start
  24.3 83.4 %all-reduce.4.cloned.1.call-done = f32[2048,512]{0,1:T(8,128)} async-done(((f32[2048,512]{0,1:T(8,128)}), f32[2048,512]{0,1:T(8,128)}) %all-reduce.4.cloned.1.call-update) | async-done | bytes 4194320 | tf_op jit(solution)/shard_map/psum | solution.py:33
  107.6 10.2 %fusion.84 = f32[512,512]{0,1:T(8,128)} fusion(f32[2048,512]{0,1:T(8,128)} %all-reduce.4.cloned.1.call-done), kind=kOutput, calls=%fused_computation.111 | convolution fusion | flops 6442450944 | bytes 5242880 | tf_op jit(solution)/shard_map/dot_general | solution.py:34
  118.0 52.0 %all-reduce.6.cloned.1.call-done = f32[512,512]{0,1:T(8,128)} async-done(((f32[512,512]{0,1:T(8,128)}), f32[512,512]{0,1:T(8,128)}) %all-reduce.6.cloned.1.call-update) | async-done | bytes 1048592 | tf_op jit(solution)/shard_map/psum | solution.py:40
  170.0 1.6 copy.6
  171.6 1.4 fusion.53
  173.0 11.7 %cholesky.104 = f32[128,128]{1,0:T(8,128)S(1)} custom-call(f32[128,128]{1,0:T(8,128)S(1)} %cholesky.266), custom_call_target="Cholesky" | custom-call | tf_op jit(solution)/shard_map/jit(cholesky)/cholesky | solution.py:41
  184.8 9.8 %custom-call.30 = f32[1,128,128]{1,2,0:T(8,128)S(1)} custom-call(f32[1,128,128]{2,1,0:T(8,128)S(1)} %get-tuple-element.32), custom_call_target="InvertDiagBlocksLowerTriangular" | custom-call | tf_op jit(solution)/shard_map/jit(cholesky)/cholesky | solution.py:41
  194.6 0.1 cholesky.224
  194.7 0.3 constant_dynamic-update-slice_fusion.3
  195.1 0.3 convolution_subtract_fusion.2
  195.4 11.7 %cholesky.217 = f32[128,128]{1,0:T(8,128)S(1)} custom-call(f32[128,128]{1,0:T(8,128)S(1)} %cholesky.270), custom_call_target="Cholesky" | custom-call | tf_op jit(solution)/shard_map/jit(cholesky)/cholesky | solution.py:41
  207.2 18.5 %custom-call.31 = f32[1,128,128]{1,2,0:T(8,128)S(1)} custom-call(f32[1,128,128]{2,1,0:T(8,128)S(1)} %get-tuple-element.29), custom_call_target="InvertDiagBlocksLowerTriangular" | custom-call | tf_op jit(solution)/shard_map/jit(cholesky)/cholesky | solution.py:41
  225.7 0.3 convolution_dynamic-update-slice_fusion
  225.9 0.4 convolution_subtract_fusion.3
  226.3 11.7 %cholesky.238 = f32[128,128]{1,0:T(8,128)S(1)} custom-call(f32[128,128]{1,0:T(8,128)S(1)} %cholesky.275), custom_call_target="Cholesky" | custom-call | tf_op jit(solution)/shard_map/jit(cholesky)/cholesky | solution.py:41
  238.1 0.7 compare_reduce_fusion.1
  238.7 9.8 %custom-call.32 = f32[1,128,128]{1,2,0:T(8,128)S(1)} custom-call(f32[1,128,128]{2,1,0:T(8,128)S(1)} %get-tuple-element.26), custom_call_target="InvertDiagBlocksLowerTriangular" | custom-call | tf_op jit(solution)/shard_map/jit(cholesky)/cholesky | solution.py:41
  248.6 0.2 convolution_dynamic-update-slice_fusion.1
  248.8 0.4 convolution_subtract_fusion.4
  249.2 11.7 %cholesky.255 = f32[128,128]{1,0:T(8,128)S(1)} custom-call(f32[128,128]{1,0:T(8,128)S(1)} %convolution_subtract_fusion.4), custom_call_target="Cholesky" | custom-call | tf_op jit(solution)/shard_map/jit(cholesky)/cholesky | solution.py:41
  260.9 0.7 compare_reduce_fusion
  261.6 0.7 compare_reduce_fusion.2
  264.8 0.3 select_select_fusion
  265.1 7.8 %while.1 = (s32[]{:T(128)}, f32[512,512]{1,0:T(8,128)S(1)}, s32[4,2]{0,1:T(2,128)S(1)}, f32[4,128,128]{2,1,0:T(8,128)S(1)}, s32[]{:T(128)}) while((s32[]{:T(128)}, f32[512,512]{1,0:T(8,128)S(1)}, s32[4,2]{0,1:T(2,128)S(1)}, f32[4,128,128]{2,1,0:T(8,128)S(1)}, s32[]{:T(128)}) %tuple.30), condition=%wide.while_cond, body=%wide.while_body.sunk | while | flops 2 | bytes 131189 | solution.py:42
  265.2 0.1 constant_dynamic-slice_fusion.2
  265.2 0.5 fusion.93
  265.8 1.3 bitcast_dynamic-update-slice_fusion.2
  267.1 0.1 constant_dynamic-slice_fusion.2
  267.2 0.5 fusion.93
  267.7 1.3 bitcast_dynamic-update-slice_fusion.2
  269.1 0.1 constant_dynamic-slice_fusion.2
  269.1 0.5 fusion.93
  269.7 1.3 bitcast_dynamic-update-slice_fusion.2
  271.0 0.1 constant_dynamic-slice_fusion.2
  271.1 0.5 fusion.93
  271.6 1.3 bitcast_dynamic-update-slice_fusion.2
  273.0 39.3 %custom-call.33 = f32[4,128,128]{1,2,0:T(8,128)S(1)} custom-call(f32[4,128,128]{2,1,0:T(8,128)S(1)} %get-tuple-element.12), custom_call_target="InvertDiagBlocksLowerTriangular" | custom-call | tf_op jit(solution)/shard_map/triangular_solve | solution.py:42
  312.3 2.5 fusion.83
  314.8 2.3 convolution_subtract_fusion.1
  317.1 1.1 fusion.82
  318.2 1.3 convolution_subtract_fusion
  319.5 1.1 fusion.81
  320.6 2.2 fusion.38
  322.8 1.1 convolution_convert_fusion
  323.9 12.6 %fusion.13 = bf16[512,1,3584]{2,0,1:T(8,128)(2,1)} fusion(bf16[1,2048,3584]{2,1,0:T(8,128)(2,1)} %param.2, bf16[2048,128]{0,1:T(8,128)(2,1)S(1)} %convolution_convert_fusion, bf16[2048,128]{0,1:T(8,128)(2,1)S(1)} %get-tuple-element.35, bf16[2048,128]{0,1:T(8,128)(2,1)S(1)} %get-tuple-element.37, bf16[2048,128]{0,1:T(8,128)(2,1)S(1)} %get-tuple-element.39), kind=kOutput, calls=%fused_computation.15 | convolution fusion | flops 7526416384 | bytes 20447232 | tf_op jit(solution)/shard_map/dot_general | solution.py:45
  336.5 68.0 %reduce-scatter.2.cloned.1.call-done = bf16[128,1,3584]{2,0,1:T(8,128)(2,1)} async-done(((bf16[512,1,3584]{2,0,1:T(8,128)(2,1)}), bf16[128,1,3584]{2,0,1:T(8,128)(2,1)}) %reduce-scatter.2.cloned.1.call-update) | async-done | bytes 917520 | tf_op jit(solution)/shard_map/reduce_scatter | solution.py:48
  (18 shorter events, 0.3 us)
Async XLA Ops:
  6.5 101.1 %all-reduce.4.cloned.1.call-start = ((), (), s32[]{:S(2)}) async-start(), calls=%async_computation.1 | async-start | bytes 8388608 | tf_op jit(solution)/shard_map/psum | solution.py:33
  23.9 146.1 %all-reduce.6.cloned.1.call-start = ((), (), s32[]{:S(2)}) async-start(), calls=%async_computation.2 | async-start | bytes 2097152 | tf_op jit(solution)/shard_map/psum | solution.py:40
  117.9 286.6 %reduce-scatter.2.cloned.1.call-start = ((), (), s32[]{:S(2)}) async-start(), calls=%async_computation.3 | async-start | bytes 4587520 | tf_op jit(solution)/shard_map/reduce_scatter | solution.py:48
  312.3 5.9 %copy-start = (f32[2048,512]{0,1:T(8,128)S(1)}, f32[2048,512]{0,1:T(8,128)}, u32[]{:S(2)}) copy-start(f32[2048,512]{0,1:T(8,128)} %all-reduce.4.cloned.1.call-done) | copy-start | bytes 12582916
Sparse Core Ops, SparseCore 0:
  24.1 83.5 all-reduce.3
  118.0 51.9 all-reduce.5
  336.6 67.8 reduce-scatter.1
where the time goes:
time: 419 us; the launch traced here: 411 us
  waiting for transfers between devices  203 us (48%)
  other arithmetic  128 us (31%)
  matrix products  52.9 us (13%)
  between operations  16.9 us (4%)
  local copies, waits for them, and re-layouts  9.44 us (2%)
    another operation x14, other arithmetic, body(): factor = jnp.linalg.cholesky(gram)  87.2 us
    psum x1, waiting for transfers between devices, body(): sketch_rows = lax.psum(partial, 'rep')  83.4 us
    reduce_scatter x1, waiting for transfers between devices, body(): lax.psum_scatter(partial_sum, 'shard', scatter_dimension=0, tiled=True)  68 us
    psum x1, waiting for transfers between devices, body(): gram = lax.psum(local_gram, 'shard')  52 us
    another operation x3, other arithmetic, body(): lax.linalg.triangular_solve(factor, sketch_rows, left_side=False, lower=T...  39.7 us
    dot_general x1, matrix products, body(): partial = jnp.dot(g, table, preferred_element_type=jnp.float32)  16.7 us
    dot_general x1, matrix products, body(): partial_sum = jnp.dot(basis_rows.T, g, preferred_element_type=jnp.float32)  12.6 us
    another operation x7, matrix products, body(): lax.linalg.triangular_solve(factor, sketch_rows, left_side=False, lower=T...  11.5 us
  transfers between devices with their start and end apart: 3, of which 3 were waited for; matrix products, arithmetic and copies ran while one was open for 0% of the time, Pallas kernels for 0%

commit v1 on v0

--- a/solution.py
+++ b/solution.py
@@ -37,7 +37,9 @@
             precision=lax.Precision.HIGHEST,
             preferred_element_type=jnp.float32,
         )
-        gram = lax.psum(local_gram, "shard")
+        gram = local_gram
+        for hop in (1, 2):
+            gram = gram + lax.ppermute(gram, "shard", [(dev, dev ^ hop) for dev in range(4)])
         factor = jnp.linalg.cholesky(gram)
         basis_rows = lax.linalg.triangular_solve(
             factor, sketch_rows, left_side=False, lower=True, transpose_a=True

time: 419 us -> 437 us (1.043)
  waiting for transfers between devices: 203 us -> 220 us
    ppermute x0 -> x2, waiting for transfers between devices: none -> 67.9 us  [body(): lax.ppermute(gram, 'shard', [(dev, dev ^ hop) for dev in range(4)])]
    psum x1 -> x0, waiting for transfers between devices: 52 us -> none  [body(): gram = lax.psum(local_gram, 'shard')]
  transfers between devices with their start and end apart: 3 -> 4, of which waited for: 3 -> 4; matrix products, arithmetic and copies ran while one was open for 0% -> 0% of each run, Pallas kernels for 0% -> 0%
where the time goes in v1:
time: 437 us; the launch traced here: 430 us
  waiting for transfers between devices  220 us (50%)
  other arithmetic  127 us (29%)
  matrix products  52 us (12%)
  between operations  17.2 us (4%)
  local copies, waits for them, and re-layouts  8.22 us (2%)
    another operation x14, other arithmetic, body(): factor = jnp.linalg.cholesky(gram)  87.3 us
    psum x1, waiting for transfers between devices, body(): sketch_rows = lax.psum(partial, 'rep')  83.4 us
    reduce_scatter x1, waiting for transfers between devices, body(): lax.psum_scatter(partial_sum, 'shard', scatter_dimension=0, tiled=True)  69 us
    ppermute x2, waiting for transfers between devices, body(): lax.ppermute(gram, 'shard', [(dev, dev ^ hop) for dev in range(4)])  67.9 us
    another operation x3, other arithmetic, body(): lax.linalg.triangular_solve(factor, sketch_rows, left_side=False, lower=T...  39.4 us
    dot_general x1, matrix products, body(): partial = jnp.dot(g, table, preferred_element_type=jnp.float32)  16.7 us
    dot_general x1, matrix products, body(): partial_sum = jnp.dot(basis_rows.T, g, preferred_element_type=jnp.float32)  12.6 us
    another operation x7, matrix products, body(): lax.linalg.triangular_solve(factor, sketch_rows, left_side=False, lower=T...  11.5 us
  transfers between devices with their start and end apart: 4, of which 4 were waited for; matrix products, arithmetic and copies ran while one was open for 0% of the time, Pallas kernels for 0%

profile of v1, /device:TPU:0, one launch (start us, length us, event | category | flops | bytes accessed | tf_op | source)
XLA Modules:
  0.0 429.6 jit_solution(8317021610807895868)
XLA Ops:
  7.2 16.7 %fusion.27 = f32[2048,512]{0,1:T(8,128)} fusion(bf16[1,2048,3584]{2,1,0:T(8,128)(2,1)} %param.2, s32[]{:T(128)} %bitcast, s32[3584]{0:T(1024)S(1)} %add_multiply_fusion), kind=kOutput, calls=%fused_computation.26 | convolution fusion | flops 7540047872 | bytes 18888708 | tf_op jit(solution)/shard_map/dot_general | solution.py:32
  23.9 0.3 reduce-scatter.2.cloned.1.call-start
  24.3 83.4 %all-reduce.3.cloned.1.call-done = f32[2048,512]{0,1:T(8,128)} async-done(((f32[2048,512]{0,1:T(8,128)}), f32[2048,512]{0,1:T(8,128)}) %all-reduce.3.cloned.1.call-update) | async-done | bytes 4194320 | tf_op jit(solution)/shard_map/psum | solution.py:33
  107.6 9.3 %fusion.89 = f32[512,512]{0,1:T(8,128)S(1)} fusion(f32[2048,512]{0,1:T(8,128)} %all-reduce.3.cloned.1.call-done), kind=kOutput, calls=%fused_computation.114 | convolution fusion | flops 6442450944 | bytes 5242880 | tf_op jit(solution)/shard_map/dot_general | solution.py:34
  116.9 1.6 collective-permute-start
  118.5 23.2 %collective-permute-done = f32[512,512]{0,1:T(8,128)S(1)} collective-permute-done((f32[512,512]{0,1:T(8,128)S(1)}, f32[512,512]{0,1:T(8,128)S(1)}, u32[]{:S(2)}, u32[]{:S(2)}) %collective-permute-start) | collective-permute-done | bytes 1048608 | tf_op jit(solution)/shard_map/ppermute | solution.py:42
  141.6 0.2 add.110
  141.9 2.5 collective-permute-start.1
  144.3 44.8 %collective-permute-done.1 = f32[512,512]{0,1:T(8,128)S(1)} collective-permute-done((f32[512,512]{0,1:T(8,128)S(1)}, f32[512,512]{0,1:T(8,128)S(1)}, u32[]{:S(2)}, u32[]{:S(2)}) %collective-permute-start.1) | collective-permute-done | bytes 1048608 | tf_op jit(solution)/shard_map/ppermute | solution.py:42
  189.1 0.2 add.111
  189.3 0.3 copy.8
  189.7 0.2 fusion.53
  189.9 11.7 %cholesky.104 = f32[128,128]{1,0:T(8,128)S(1)} custom-call(f32[128,128]{1,0:T(8,128)S(1)} %cholesky.266), custom_call_target="Cholesky" | custom-call | tf_op jit(solution)/shard_map/jit(cholesky)/cholesky | solution.py:43
  201.7 9.8 %custom-call.30 = f32[1,128,128]{1,2,0:T(8,128)S(1)} custom-call(f32[1,128,128]{2,1,0:T(8,128)S(1)} %get-tuple-element.32), custom_call_target="InvertDiagBlocksLowerTriangular" | custom-call | tf_op jit(solution)/shard_map/jit(cholesky)/cholesky | solution.py:43
  211.6 0.3 constant_dynamic-update-slice_fusion.3
  211.9 0.3 slice_subtract_fusion
  212.3 11.7 %cholesky.217 = f32[128,128]{1,0:T(8,128)S(1)} custom-call(f32[128,128]{1,0:T(8,128)S(1)} %cholesky.270), custom_call_target="Cholesky" | custom-call | tf_op jit(solution)/shard_map/jit(cholesky)/cholesky | solution.py:43
  224.0 18.5 %custom-call.31 = f32[1,128,128]{1,2,0:T(8,128)S(1)} custom-call(f32[1,128,128]{2,1,0:T(8,128)S(1)} %get-tuple-element.29), custom_call_target="InvertDiagBlocksLowerTriangular" | custom-call | tf_op jit(solution)/shard_map/jit(cholesky)/cholesky | solution.py:43
  242.5 0.3 convolution_dynamic-update-slice_fusion
  242.8 0.4 slice_subtract_fusion.1
  243.2 11.7 %cholesky.238 = f32[128,128]{1,0:T(8,128)S(1)} custom-call(f32[128,128]{1,0:T(8,128)S(1)} %cholesky.275), custom_call_target="Cholesky" | custom-call | tf_op jit(solution)/shard_map/jit(cholesky)/cholesky | solution.py:43
  254.9 0.7 compare_reduce_fusion.1
  255.6 9.8 %custom-call.32 = f32[1,128,128]{1,2,0:T(8,128)S(1)} custom-call(f32[1,128,128]{2,1,0:T(8,128)S(1)} %get-tuple-element.26), custom_call_target="InvertDiagBlocksLowerTriangular" | custom-call | tf_op jit(solution)/shard_map/jit(cholesky)/cholesky | solution.py:43
  265.4 0.2 convolution_dynamic-update-slice_fusion.1
  265.6 0.4 slice_subtract_fusion.2
  266.0 11.9 %cholesky.255 = f32[128,128]{1,0:T(8,128)S(1)} custom-call(f32[128,128]{1,0:T(8,128)S(1)} %slice_subtract_fusion.2), custom_call_target="Cholesky" | custom-call | tf_op jit(solution)/shard_map/jit(cholesky)/cholesky | solution.py:43
  277.9 0.7 compare_reduce_fusion
  278.6 0.7 compare_reduce_fusion.2
  281.8 0.1 select_select_fusion
  282.0 7.8 %while.1 = (s32[]{:T(128)}, f32[512,512]{1,0:T(8,128)S(1)}, s32[4,2]{0,1:T(2,128)S(1)}, f32[4,128,128]{2,1,0:T(8,128)S(1)}, s32[]{:T(128)}) while((s32[]{:T(128)}, f32[512,512]{1,0:T(8,128)S(1)}, s32[4,2]{0,1:T(2,128)S(1)}, f32[4,128,128]{2,1,0:T(8,128)S(1)}, s32[]{:T(128)}) %tuple.30), condition=%wide.while_cond, body=%wide.while_body.sunk | while | flops 2 | bytes 131189 | solution.py:44
  282.0 0.5 fusion.98
  282.6 1.3 bitcast_dynamic-update-slice_fusion.2
  284.0 0.5 fusion.98
  284.5 1.3 bitcast_dynamic-update-slice_fusion.2
  286.0 0.5 fusion.98
  286.5 1.3 bitcast_dynamic-update-slice_fusion.2
  287.9 0.5 fusion.98
  288.5 1.3 bitcast_dynamic-update-slice_fusion.2
  289.8 39.3 %custom-call.33 = f32[4,128,128]{1,2,0:T(8,128)S(1)} custom-call(f32[4,128,128]{2,1,0:T(8,128)S(1)} %get-tuple-element.12), custom_call_target="InvertDiagBlocksLowerTriangular" | custom-call | tf_op jit(solution)/shard_map/triangular_solve | solution.py:44
  329.1 2.5 fusion.88
  331.6 2.3 convolution_subtract_fusion.1
  333.9 1.1 fusion.87
  335.0 1.3 convolution_subtract_fusion
  336.3 1.1 fusion.86
  337.4 2.2 fusion.38
  339.6 1.1 convolution_convert_fusion
  340.7 12.6 %fusion.13 = bf16[512,1,3584]{2,0,1:T(8,128)(2,1)} fusion(bf16[1,2048,3584]{2,1,0:T(8,128)(2,1)} %param.2, bf16[2048,128]{0,1:T(8,128)(2,1)S(1)} %convolution_convert_fusion, bf16[2048,128]{0,1:T(8,128)(2,1)S(1)} %get-tuple-element.35, bf16[2048,128]{0,1:T(8,128)(2,1)S(1)} %get-tuple-element.37, bf16[2048,128]{0,1:T(8,128)(2,1)S(1)} %get-tuple-element.39), kind=kOutput, calls=%fused_computation.15 | convolution fusion | flops 7526416384 | bytes 20447232 | tf_op jit(solution)/shard_map/dot_general | solution.py:47
  353.3 69.0 %reduce-scatter.2.cloned.1.call-done = bf16[128,1,3584]{2,0,1:T(8,128)(2,1)} async-done(((bf16[512,1,3584]{2,0,1:T(8,128)(2,1)}), bf16[128,1,3584]{2,0,1:T(8,128)(2,1)}) %reduce-scatter.2.cloned.1.call-update) | async-done | bytes 917520 | tf_op jit(solution)/shard_map/reduce_scatter | solution.py:50
  (21 shorter events, 0.6 us)
Async XLA Ops:
  6.5 101.1 %all-reduce.3.cloned.1.call-start = ((), (), s32[]{:S(2)}) async-start(), calls=%async_computation.1 | async-start | bytes 8388608 | tf_op jit(solution)/shard_map/psum | solution.py:33
  23.9 398.4 %reduce-scatter.2.cloned.1.call-start = ((), (), s32[]{:S(2)}) async-start(), calls=%async_computation.2 | async-start | bytes 4587520 | tf_op jit(solution)/shard_map/reduce_scatter | solution.py:50
  116.9 24.7 %collective-permute-start = (f32[512,512]{0,1:T(8,128)S(1)}, f32[512,512]{0,1:T(8,128)S(1)}, u32[]{:S(2)}, u32[]{:S(2)}) collective-permute-start(f32[512,512]{0,1:T(8,128)S(1)} %fusion.89), channel_id=1, source_target_pairs={{0,8},{8,0},{16,24},{24,16},{1,9},{9,1},{17,25},{25,17},{2,10},{10... | collective-permute-start | bytes 3145736 | tf_op jit(solution)/shard_map/ppermute | solution.py:42
  141.9 47.2 %collective-permute-start.1 = (f32[512,512]{0,1:T(8,128)S(1)}, f32[512,512]{0,1:T(8,128)S(1)}, u32[]{:S(2)}, u32[]{:S(2)}) collective-permute-start(f32[512,512]{0,1:T(8,128)S(1)} %add.110), channel_id=1, source_target_pairs={{0,16},{8,24},{16,0},{24,8},{1,17},{9,25},{17,1},{25,9},{2,18},{10... | collective-permute-start | bytes 3145736 | tf_op jit(solution)/shard_map/ppermute | solution.py:42
  329.1 5.9 %copy-start = (f32[2048,512]{0,1:T(8,128)S(1)}, f32[2048,512]{0,1:T(8,128)}, u32[]{:S(2)}) copy-start(f32[2048,512]{0,1:T(8,128)} %all-reduce.3.cloned.1.call-done) | copy-start | bytes 12582916
Sparse Core Ops, SparseCore 0:
  24.1 83.5 all-reduce.2
  353.4 68.8 reduce-scatter.1
